TPU v7x, 128 devices: a whole 4x4x4 slice. The times are simulated.
128 devices in a mesh: gx: 8 (over z, core), gy: 16 (over y, x).
Axes of the slice: x: 4, y: 4, z: 4, core: 2. Of those that a mesh axis runs over, the one named last changes fastest.
Arguments:
- hidden_in: bfloat16 [32768, 3584], P(('gx', 'gy')), may hold values from -6 to 6
- lengths: int32 [8, 4], P('gx'), may hold values from 1 to 2048, 4096 in all within a row
- attn_norm: float32 [3584], replicated, may hold values from 0.5 to 1.5
- qkv_weight: bfloat16 [3584, 4608], P('gx', 'gy'), may hold values from -0.09375 to 0.09375
- qkv_bias: float32 [4608], replicated, may hold values from -5 to 5
Outputs:
- attn: bfloat16 [32768, 3584], P(('gx', 'gy'))
- kv_rows: bfloat16 [32768, 1024], P(('gx', 'gy'))
Inputs may be any that keep to these rules, and one draw needn't show every extreme that they name: Each row of lengths sums to 4096; the longest of each row is exactly 2048.
All inputs are finite; a program needn't handle non-finite values.
Results may differ from a plain program's by a relative error of at most 0.0035.
The roundings to bfloat16 on the way count: a program that leaves them out, or rounds other values in their place, can miss the bound.
Values may be sent and summed in bfloat16 or wider, within the bound.
No kernel may reach another device: no remote copies, remote signals or barrier semaphores. Data moves between devices by JAX's collectives and lax.ppermute only.
A program may use at most 128 MiB of HBM per device.

v0:
```python
import math

import jax
import jax.numpy as jnp
from jax import lax
from jax.sharding import PartitionSpec as P

HEADS = 28
KV_HEADS = 4
HEAD_DIM = 128


key_span = 512


def norm_rows(values, gain):
    wide = values.astype(jnp.float32)
    scale = lax.rsqrt(jnp.mean(wide * wide, axis=1, keepdims=True) + 1e-06)
    return (wide * scale * gain[None, :]).astype(jnp.bfloat16)


def segment_of(index, ends):
    return jnp.sum((ends[None, :] <= index[:, None]).astype(jnp.int32), axis=1)


def rotate(block, pos, heads):
    half = HEAD_DIM // 2
    freqs = 1000000.0 ** (-2.0 * jnp.arange(half, dtype=jnp.float32) / HEAD_DIM)
    angle = pos.astype(jnp.float32)[:, None, None] * freqs[None, None, :]
    wide = block.astype(jnp.float32).reshape(block.shape[0], heads, HEAD_DIM)
    first, second = (wide[..., :half], wide[..., half:])
    turned = jnp.concatenate(
        [
            first * jnp.cos(angle) - second * jnp.sin(angle),
            second * jnp.cos(angle) + first * jnp.sin(angle),
        ],
        axis=2,
    )
    return turned.reshape(block.shape[0], heads * HEAD_DIM).astype(jnp.bfloat16)


def project_joined(normed, weight, bias):
    grouped = lax.all_gather(normed, "gy", axis=0, tiled=True)
    summed = jnp.dot(
        grouped,
        lax.all_gather(weight, "gx", axis=0, tiled=True),
        preferred_element_type=jnp.float32,
    )
    width = weight.shape[1]
    bias_block = lax.dynamic_slice_in_dim(bias, lax.axis_index("gy") * width, width, 0)
    block_out = (summed + bias_block[None, :]).astype(jnp.bfloat16)
    return lax.all_to_all(block_out, "gy", split_axis=0, concat_axis=1, tiled=True)


def on_device(hidden_in, lengths, attn_norm, qkv_weight, qkv_bias):
    rows = hidden_in.shape[0]
    first = lax.axis_index("gy") * rows
    row_lengths = lengths[0]
    qdim = HEADS * HEAD_DIM
    kdim = KV_HEADS * HEAD_DIM
    group = HEADS // KV_HEADS
    normed = norm_rows(hidden_in, attn_norm)
    joined = project_joined(normed, qkv_weight, qkv_bias)
    ends = jnp.cumsum(row_lengths)
    tokens_here = first + jnp.arange(rows, dtype=jnp.int32)
    before = ends[None, :] <= tokens_here[:, None]
    seg_here = jnp.sum(before.astype(jnp.int32), axis=1)
    begin = jnp.sum(jnp.where(before, row_lengths[None, :], 0), axis=1)
    pos = tokens_here - begin
    queries = rotate(joined[:, :qdim], pos, HEADS).reshape(rows, KV_HEADS, group, HEAD_DIM)
    keys = rotate(joined[:, qdim : qdim + kdim], pos, KV_HEADS)
    kv_rows = jnp.concatenate([keys, joined[:, qdim + kdim :]], axis=1)
    scale = 1.0 / HEAD_DIM**0.5

    def attend(carry, piece, start):
        running, total, summed = carry
        key_count = piece.shape[0]
        key_index = start + jnp.arange(key_count, dtype=jnp.int32)
        key_seg = segment_of(key_index, ends)
        key_part = piece[:, :kdim].reshape(key_count, KV_HEADS, HEAD_DIM)
        value_part = piece[:, kdim:].reshape(key_count, KV_HEADS, HEAD_DIM)
        scores = (
            jnp.einsum("rgho,ngo->ghrn", queries, key_part, preferred_element_type=jnp.float32)
            * scale
        )
        allowed = (seg_here[:, None] == key_seg[None, :]) & (
            key_index[None, :] <= tokens_here[:, None]
        )
        newest = jnp.maximum(running, jnp.max(jnp.where(allowed, scores, -1e30), axis=3))
        shrink = jnp.exp(running - newest)
        weights = jnp.where(allowed, jnp.exp(scores - newest[..., None]), 0.0)
        total = total * shrink + jnp.sum(weights, axis=3)
        summed = summed * shrink[..., None] + jnp.einsum(
            "ghrn,ngo->ghro",
            weights.astype(jnp.bfloat16),
            value_part,
            preferred_element_type=jnp.float32,
        )
        return (newest, total, summed)

    def visit(carry, piece, start):
        return attend(carry, piece, start)

    start_state = (
        jnp.full((KV_HEADS, group, rows), -1e30, jnp.float32),
        jnp.zeros((KV_HEADS, group, rows), jnp.float32),
        jnp.zeros((KV_HEADS, group, rows, HEAD_DIM), jnp.float32),
    )
    piece = lax.all_gather(kv_rows, "gy", axis=0, tiled=True)
    length = piece.shape[0]
    span = math.gcd(length, key_span)
    stacked = piece.reshape(length // span, span, piece.shape[1])
    offsets = jnp.arange(length // span, dtype=jnp.int32) * span

    def advance(state, item):
        return (visit(state, item[0], item[1]), None)

    final_state, unused = lax.scan(advance, start_state, (stacked, offsets))
    running, total, summed = final_state
    attn = (
        jnp.transpose(summed / total[..., None], (2, 0, 1, 3))
        .reshape(rows, qdim)
        .astype(jnp.bfloat16)
    )
    return (attn, kv_rows)


def solution(mesh):
    placed = (P(("gx", "gy"), None), P("gx", None), P(), P("gx", "gy"), P())
    return jax.shard_map(
        on_device,
        mesh=mesh,
        in_specs=placed,
        out_specs=(P(("gx", "gy"), None), P(("gx", "gy"), None)),
        check_vma=False,
    )
```

profile of v0, /device:TPU:28, one launch (start us, length us, event | category | flops | bytes accessed | tf_op | source)
XLA Modules:
  0.0 593.0 jit_solution(592481126304964280)
XLA Ops:
  13.9 23.6 %all-gather.9.cloned.1.call-done = bf16[8,448,288]{1,2,0:T(8,128)(2,1)} async-done(((bf16[1,448,288]{1,2,0:T(8,128)(2,1)}), bf16[8,448,288]{1,2,0:T(8,128)(2,1)}) %all-gather.9.cloned.1.call-update) | async-done | bytes 2064400 | tf_op jit(solution)/shard_map/all_gather | solution.py:46
  44.1 170.5 %all-gather.5.cloned.1.call-done = bf16[4096,3584]{1,0:T(8,128)(2,1)} async-done(((bf16[256,3584]{1,0:T(8,128)(2,1)}), bf16[4096,3584]{1,0:T(8,128)(2,1)}) %all-gather.5.cloned.1.call-update) | async-done | bytes 29360144 | tf_op jit(solution)/shard_map/all_gather | solution.py:43
  214.6 14.7 %fusion.16 = bf16[4096,288]{0,1:T(8,128)(2,1)S(1)} fusion(bf16[4096,3584]{1,0:T(8,128)(2,1)} %all-gather.5.cloned.1.call-done, bf16[3584,288]{0,1:T(8,128)(2,1)} %reshape.172, f32[288]{0:T(512)S(1)} %dynamic_slice.11), kind=kOutput, calls=%fused_computation.25 | convolution fusion | flops 8458076160 | bytes 33784960 | tf_op jit(solution)/shard_map/dot_general | solution.py:44
  231.0 7.2 %all-to-all-start = ((bf16[16,256,288]{1,2,0:T(8,128)(2,1)}), bf16[16,256,288]{1,2,0:T(8,128)(2,1)S(1)}, u32[]{:S(2)}, u32[]{:S(2)}) async-start(bf16[16,256,288]{1,2,0:T(8,128)(2,1)} %bitcast.85), calls=%async_computation | async-start | bytes 4718592 | tf_op jit(solution)/shard_map/all_to_all | solution.py:52
  239.0 29.9 %all-to-all-done = bf16[16,256,288]{1,2,0:T(8,128)(2,1)S(1)} async-done(((bf16[16,256,288]{1,2,0:T(8,128)(2,1)}), bf16[16,256,288]{1,2,0:T(8,128)(2,1)S(1)}, u32[]{:S(2)}, u32[]{:S(2)}) %all-to-all-start) | async-done | bytes 2359328 | tf_op jit(solution)/shard_map/all_to_all | solution.py:52
  279.2 68.2 %all-gather.7.cloned.1.call-done = bf16[4096,1024]{0,1:T(8,128)(2,1)} async-done(((bf16[256,1024]{0,1:T(8,128)(2,1)}), bf16[4096,1024]{0,1:T(8,128)(2,1)}) %all-gather.7.cloned.1.call-update) | async-done | bytes 8388624 | tf_op jit(solution)/shard_map/all_gather | solution.py:109
  347.4 7.5 %copy.52 = bf16[128,8,8,512]{3,2,0,1:T(8,128)(2,1)} copy(bf16[128,8,8,512]{3,2,1,0:T(8,128)(2,1)} %bitcast.86) | data formatting | bytes 16777216 | tf_op jit(solution)/shard_map/reshape | solution.py:112
  354.9 222.0 %while.15 = (s32[]{:T(128)}, f32[4,7,256]{2,1,0:T(8,128)S(1)}, f32[4,7,256]{2,1,0:T(8,128)S(1)}, f32[4,7,256,128]{3,2,1,0:T(8,128)}, s32[256]{0:T(256)S(1)}, /*i...) while((s32[]{:T(128)}, f32[4,7,256]{2,1,0:T(8,128)S(1)}, ...), condition=%wide.region_8.9_spmd.clone, body=%wide.region_4.8_spmd.clone.sunk | while | flops 1922606336 | bytes 88814816 | solution.py:118
  357.8 6.5 %fusion.43 = (f32[4,7,256]{2,1,0:T(8,128)S(1)}, f32[4,512,256,7]{2,1,3,0:T(8,128)}) fusion(pred[256,512]{0,1:T(8,128)(4,1)S(1)} %compare_and_fusion.2, bf16[512,4,128,1]{0,2,3,1:T(8,128)(2,1)S(1)} %bitcast.80, bf16[256,4,7,128]{3,0,2,1:T(8,128)(2,1)S(1)} %get-tuple-element.270), kind=kOutput, calls=%fused_computation.3.clone.1 | convolution fusion | flops 950526976 | bytes 17199104 | tf_op jit(solution)/shard_map/while/body/eval_jaxpr/rgho,ngo->ghrn/dot_general | solution.py:83
  364.4 8.3 %fusion.44 = f32[4,7,256]{2,1,0:T(8,128)S(1)} fusion(f32[4,512,256,7]{2,1,3,0:T(8,128)} %get-tuple-element.234, f32[4,7,256]{2,1,0:T(8,128)S(1)} %select_maximum_fusion.2, pred[256,512]{0,1:T(8,128)(4,1)S(1)} %compare_and_fusion.2), kind=kLoop, calls=%fused_computation.7.clone.1 | loop fusion | flops 14672896 | bytes 14868480 | tf_op jit(solution)/shard_map/while/body/eval_jaxpr/reduce_sum | solution.py:92
  372.7 8.0 %fusion.46 = f32[4,7,256,128]{3,2,1,0:T(8,128)S(1)} fusion(f32[4,7,256,128]{3,2,1,0:T(8,128)S(1)} %copy-done.1, bf16[512,4,128,1]{0,2,3,1:T(8,128)(2,1)S(1)} %bitcast.82, f32[4,512,256,7]{2,1,3,0:T(8,128)} %get-tuple-element.234, f32[4,7,256]{2,1,0:T(8,128)S(1)} %select_maximum_fusion.2, pred[256,512]{0,1:T(8,128)(4,1)S(1)} %compare_and_fusion.2, ...), kind=kOutput, calls=%fused_computation.11.clone.1 | convolution fusion | flops 956956672 | bytes 22732800 | tf_op jit(solution)/shard_map/while/body/eval_jaxpr/ghrn,ngo->ghro/dot_general | solution.py:93
  385.6 6.5 %fusion.43 = (f32[4,7,256]{2,1,0:T(8,128)S(1)}, f32[4,512,256,7]{2,1,3,0:T(8,128)}) fusion(pred[256,512]{0,1:T(8,128)(4,1)S(1)} %compare_and_fusion.2, bf16[512,4,128,1]{0,2,3,1:T(8,128)(2,1)S(1)} %bitcast.80, bf16[256,4,7,128]{3,0,2,1:T(8,128)(2,1)S(1)} %get-tuple-element.270), kind=kOutput, calls=%fused_computation.3.clone.1 | convolution fusion | flops 950526976 | bytes 17199104 | tf_op jit(solution)/shard_map/while/body/eval_jaxpr/rgho,ngo->ghrn/dot_general | solution.py:83
  392.1 8.3 %fusion.44 = f32[4,7,256]{2,1,0:T(8,128)S(1)} fusion(f32[4,512,256,7]{2,1,3,0:T(8,128)} %get-tuple-element.234, f32[4,7,256]{2,1,0:T(8,128)S(1)} %select_maximum_fusion.2, pred[256,512]{0,1:T(8,128)(4,1)S(1)} %compare_and_fusion.2), kind=kLoop, calls=%fused_computation.7.clone.1 | loop fusion | flops 14672896 | bytes 14868480 | tf_op jit(solution)/shard_map/while/body/eval_jaxpr/reduce_sum | solution.py:92
  400.5 8.0 %fusion.46 = f32[4,7,256,128]{3,2,1,0:T(8,128)S(1)} fusion(f32[4,7,256,128]{3,2,1,0:T(8,128)S(1)} %copy-done.1, bf16[512,4,128,1]{0,2,3,1:T(8,128)(2,1)S(1)} %bitcast.82, f32[4,512,256,7]{2,1,3,0:T(8,128)} %get-tuple-element.234, f32[4,7,256]{2,1,0:T(8,128)S(1)} %select_maximum_fusion.2, pred[256,512]{0,1:T(8,128)(4,1)S(1)} %compare_and_fusion.2, ...), kind=kOutput, calls=%fused_computation.11.clone.1 | convolution fusion | flops 956956672 | bytes 22732800 | tf_op jit(solution)/shard_map/while/body/eval_jaxpr/ghrn,ngo->ghro/dot_general | solution.py:93
  413.3 6.5 %fusion.43 = (f32[4,7,256]{2,1,0:T(8,128)S(1)}, f32[4,512,256,7]{2,1,3,0:T(8,128)}) fusion(pred[256,512]{0,1:T(8,128)(4,1)S(1)} %compare_and_fusion.2, bf16[512,4,128,1]{0,2,3,1:T(8,128)(2,1)S(1)} %bitcast.80, bf16[256,4,7,128]{3,0,2,1:T(8,128)(2,1)S(1)} %get-tuple-element.270), kind=kOutput, calls=%fused_computation.3.clone.1 | convolution fusion | flops 950526976 | bytes 17199104 | tf_op jit(solution)/shard_map/while/body/eval_jaxpr/rgho,ngo->ghrn/dot_general | solution.py:83
  419.8 8.3 %fusion.44 = f32[4,7,256]{2,1,0:T(8,128)S(1)} fusion(f32[4,512,256,7]{2,1,3,0:T(8,128)} %get-tuple-element.234, f32[4,7,256]{2,1,0:T(8,128)S(1)} %select_maximum_fusion.2, pred[256,512]{0,1:T(8,128)(4,1)S(1)} %compare_and_fusion.2), kind=kLoop, calls=%fused_computation.7.clone.1 | loop fusion | flops 14672896 | bytes 14868480 | tf_op jit(solution)/shard_map/while/body/eval_jaxpr/reduce_sum | solution.py:92
  428.2 8.0 %fusion.46 = f32[4,7,256,128]{3,2,1,0:T(8,128)S(1)} fusion(f32[4,7,256,128]{3,2,1,0:T(8,128)S(1)} %copy-done.1, bf16[512,4,128,1]{0,2,3,1:T(8,128)(2,1)S(1)} %bitcast.82, f32[4,512,256,7]{2,1,3,0:T(8,128)} %get-tuple-element.234, f32[4,7,256]{2,1,0:T(8,128)S(1)} %select_maximum_fusion.2, pred[256,512]{0,1:T(8,128)(4,1)S(1)} %compare_and_fusion.2, ...), kind=kOutput, calls=%fused_computation.11.clone.1 | convolution fusion | flops 956956672 | bytes 22732800 | tf_op jit(solution)/shard_map/while/body/eval_jaxpr/ghrn,ngo->ghro/dot_general | solution.py:93
  441.0 6.5 %fusion.43 = (f32[4,7,256]{2,1,0:T(8,128)S(1)}, f32[4,512,256,7]{2,1,3,0:T(8,128)}) fusion(pred[256,512]{0,1:T(8,128)(4,1)S(1)} %compare_and_fusion.2, bf16[512,4,128,1]{0,2,3,1:T(8,128)(2,1)S(1)} %bitcast.80, bf16[256,4,7,128]{3,0,2,1:T(8,128)(2,1)S(1)} %get-tuple-element.270), kind=kOutput, calls=%fused_computation.3.clone.1 | convolution fusion | flops 950526976 | bytes 17199104 | tf_op jit(solution)/shard_map/while/body/eval_jaxpr/rgho,ngo->ghrn/dot_general | solution.py:83
  447.6 8.3 %fusion.44 = f32[4,7,256]{2,1,0:T(8,128)S(1)} fusion(f32[4,512,256,7]{2,1,3,0:T(8,128)} %get-tuple-element.234, f32[4,7,256]{2,1,0:T(8,128)S(1)} %select_maximum_fusion.2, pred[256,512]{0,1:T(8,128)(4,1)S(1)} %compare_and_fusion.2), kind=kLoop, calls=%fused_computation.7.clone.1 | loop fusion | flops 14672896 | bytes 14868480 | tf_op jit(solution)/shard_map/while/body/eval_jaxpr/reduce_sum | solution.py:92
  455.9 8.0 %fusion.46 = f32[4,7,256,128]{3,2,1,0:T(8,128)S(1)} fusion(f32[4,7,256,128]{3,2,1,0:T(8,128)S(1)} %copy-done.1, bf16[512,4,128,1]{0,2,3,1:T(8,128)(2,1)S(1)} %bitcast.82, f32[4,512,256,7]{2,1,3,0:T(8,128)} %get-tuple-element.234, f32[4,7,256]{2,1,0:T(8,128)S(1)} %select_maximum_fusion.2, pred[256,512]{0,1:T(8,128)(4,1)S(1)} %compare_and_fusion.2, ...), kind=kOutput, calls=%fused_computation.11.clone.1 | convolution fusion | flops 956956672 | bytes 22732800 | tf_op jit(solution)/shard_map/while/body/eval_jaxpr/ghrn,ngo->ghro/dot_general | solution.py:93
  468.8 6.5 %fusion.43 = (f32[4,7,256]{2,1,0:T(8,128)S(1)}, f32[4,512,256,7]{2,1,3,0:T(8,128)}) fusion(pred[256,512]{0,1:T(8,128)(4,1)S(1)} %compare_and_fusion.2, bf16[512,4,128,1]{0,2,3,1:T(8,128)(2,1)S(1)} %bitcast.80, bf16[256,4,7,128]{3,0,2,1:T(8,128)(2,1)S(1)} %get-tuple-element.270), kind=kOutput, calls=%fused_computation.3.clone.1 | convolution fusion | flops 950526976 | bytes 17199104 | tf_op jit(solution)/shard_map/while/body/eval_jaxpr/rgho,ngo->ghrn/dot_general | solution.py:83
  475.3 8.3 %fusion.44 = f32[4,7,256]{2,1,0:T(8,128)S(1)} fusion(f32[4,512,256,7]{2,1,3,0:T(8,128)} %get-tuple-element.234, f32[4,7,256]{2,1,0:T(8,128)S(1)} %select_maximum_fusion.2, pred[256,512]{0,1:T(8,128)(4,1)S(1)} %compare_and_fusion.2), kind=kLoop, calls=%fused_computation.7.clone.1 | loop fusion | flops 14672896 | bytes 14868480 | tf_op jit(solution)/shard_map/while/body/eval_jaxpr/reduce_sum | solution.py:92
  483.7 8.0 %fusion.46 = f32[4,7,256,128]{3,2,1,0:T(8,128)S(1)} fusion(f32[4,7,256,128]{3,2,1,0:T(8,128)S(1)} %copy-done.1, bf16[512,4,128,1]{0,2,3,1:T(8,128)(2,1)S(1)} %bitcast.82, f32[4,512,256,7]{2,1,3,0:T(8,128)} %get-tuple-element.234, f32[4,7,256]{2,1,0:T(8,128)S(1)} %select_maximum_fusion.2, pred[256,512]{0,1:T(8,128)(4,1)S(1)} %compare_and_fusion.2, ...), kind=kOutput, calls=%fused_computation.11.clone.1 | convolution fusion | flops 956956672 | bytes 22732800 | tf_op jit(solution)/shard_map/while/body/eval_jaxpr/ghrn,ngo->ghro/dot_general | solution.py:93
  496.5 6.5 %fusion.43 = (f32[4,7,256]{2,1,0:T(8,128)S(1)}, f32[4,512,256,7]{2,1,3,0:T(8,128)}) fusion(pred[256,512]{0,1:T(8,128)(4,1)S(1)} %compare_and_fusion.2, bf16[512,4,128,1]{0,2,3,1:T(8,128)(2,1)S(1)} %bitcast.80, bf16[256,4,7,128]{3,0,2,1:T(8,128)(2,1)S(1)} %get-tuple-element.270), kind=kOutput, calls=%fused_computation.3.clone.1 | convolution fusion | flops 950526976 | bytes 17199104 | tf_op jit(solution)/shard_map/while/body/eval_jaxpr/rgho,ngo->ghrn/dot_general | solution.py:83
  503.1 8.3 %fusion.44 = f32[4,7,256]{2,1,0:T(8,128)S(1)} fusion(f32[4,512,256,7]{2,1,3,0:T(8,128)} %get-tuple-element.234, f32[4,7,256]{2,1,0:T(8,128)S(1)} %select_maximum_fusion.2, pred[256,512]{0,1:T(8,128)(4,1)S(1)} %compare_and_fusion.2), kind=kLoop, calls=%fused_computation.7.clone.1 | loop fusion | flops 14672896 | bytes 14868480 | tf_op jit(solution)/shard_map/while/body/eval_jaxpr/reduce_sum | solution.py:92
  511.4 8.0 %fusion.46 = f32[4,7,256,128]{3,2,1,0:T(8,128)S(1)} fusion(f32[4,7,256,128]{3,2,1,0:T(8,128)S(1)} %copy-done.1, bf16[512,4,128,1]{0,2,3,1:T(8,128)(2,1)S(1)} %bitcast.82, f32[4,512,256,7]{2,1,3,0:T(8,128)} %get-tuple-element.234, f32[4,7,256]{2,1,0:T(8,128)S(1)} %select_maximum_fusion.2, pred[256,512]{0,1:T(8,128)(4,1)S(1)} %compare_and_fusion.2, ...), kind=kOutput, calls=%fused_computation.11.clone.1 | convolution fusion | flops 956956672 | bytes 22732800 | tf_op jit(solution)/shard_map/while/body/eval_jaxpr/ghrn,ngo->ghro/dot_general | solution.py:93
  524.3 6.5 %fusion.43 = (f32[4,7,256]{2,1,0:T(8,128)S(1)}, f32[4,512,256,7]{2,1,3,0:T(8,128)}) fusion(pred[256,512]{0,1:T(8,128)(4,1)S(1)} %compare_and_fusion.2, bf16[512,4,128,1]{0,2,3,1:T(8,128)(2,1)S(1)} %bitcast.80, bf16[256,4,7,128]{3,0,2,1:T(8,128)(2,1)S(1)} %get-tuple-element.270), kind=kOutput, calls=%fused_computation.3.clone.1 | convolution fusion | flops 950526976 | bytes 17199104 | tf_op jit(solution)/shard_map/while/body/eval_jaxpr/rgho,ngo->ghrn/dot_general | solution.py:83
  530.8 8.3 %fusion.44 = f32[4,7,256]{2,1,0:T(8,128)S(1)} fusion(f32[4,512,256,7]{2,1,3,0:T(8,128)} %get-tuple-element.234, f32[4,7,256]{2,1,0:T(8,128)S(1)} %select_maximum_fusion.2, pred[256,512]{0,1:T(8,128)(4,1)S(1)} %compare_and_fusion.2), kind=kLoop, calls=%fused_computation.7.clone.1 | loop fusion | flops 14672896 | bytes 14868480 | tf_op jit(solution)/shard_map/while/body/eval_jaxpr/reduce_sum | solution.py:92
  539.2 8.0 %fusion.46 = f32[4,7,256,128]{3,2,1,0:T(8,128)S(1)} fusion(f32[4,7,256,128]{3,2,1,0:T(8,128)S(1)} %copy-done.1, bf16[512,4,128,1]{0,2,3,1:T(8,128)(2,1)S(1)} %bitcast.82, f32[4,512,256,7]{2,1,3,0:T(8,128)} %get-tuple-element.234, f32[4,7,256]{2,1,0:T(8,128)S(1)} %select_maximum_fusion.2, pred[256,512]{0,1:T(8,128)(4,1)S(1)} %compare_and_fusion.2, ...), kind=kOutput, calls=%fused_computation.11.clone.1 | convolution fusion | flops 956956672 | bytes 22732800 | tf_op jit(solution)/shard_map/while/body/eval_jaxpr/ghrn,ngo->ghro/dot_general | solution.py:93
  552.0 6.5 %fusion.43 = (f32[4,7,256]{2,1,0:T(8,128)S(1)}, f32[4,512,256,7]{2,1,3,0:T(8,128)}) fusion(pred[256,512]{0,1:T(8,128)(4,1)S(1)} %compare_and_fusion.2, bf16[512,4,128,1]{0,2,3,1:T(8,128)(2,1)S(1)} %bitcast.80, bf16[256,4,7,128]{3,0,2,1:T(8,128)(2,1)S(1)} %get-tuple-element.270), kind=kOutput, calls=%fused_computation.3.clone.1 | convolution fusion | flops 950526976 | bytes 17199104 | tf_op jit(solution)/shard_map/while/body/eval_jaxpr/rgho,ngo->ghrn/dot_general | solution.py:83
  558.6 8.3 %fusion.44 = f32[4,7,256]{2,1,0:T(8,128)S(1)} fusion(f32[4,512,256,7]{2,1,3,0:T(8,128)} %get-tuple-element.234, f32[4,7,256]{2,1,0:T(8,128)S(1)} %select_maximum_fusion.2, pred[256,512]{0,1:T(8,128)(4,1)S(1)} %compare_and_fusion.2), kind=kLoop, calls=%fused_computation.7.clone.1 | loop fusion | flops 14672896 | bytes 14868480 | tf_op jit(solution)/shard_map/while/body/eval_jaxpr/reduce_sum | solution.py:92
  566.9 8.0 %fusion.46 = f32[4,7,256,128]{3,2,1,0:T(8,128)S(1)} fusion(f32[4,7,256,128]{3,2,1,0:T(8,128)S(1)} %copy-done.1, bf16[512,4,128,1]{0,2,3,1:T(8,128)(2,1)S(1)} %bitcast.82, f32[4,512,256,7]{2,1,3,0:T(8,128)} %get-tuple-element.234, f32[4,7,256]{2,1,0:T(8,128)S(1)} %select_maximum_fusion.2, pred[256,512]{0,1:T(8,128)(4,1)S(1)} %compare_and_fusion.2, ...), kind=kOutput, calls=%fused_computation.11.clone.1 | convolution fusion | flops 956956672 | bytes 22732800 | tf_op jit(solution)/shard_map/while/body/eval_jaxpr/ghrn,ngo->ghro/dot_general | solution.py:93
  (153 shorter events, 74.1 us)
Async XLA Ops:
  7.2 30.4 %all-gather.9.cloned.1.call-start = ((), (), s32[]{:S(2)}) async-start(), calls=%async_computation.3 | async-start | bytes 2654208 | tf_op jit(solution)/shard_map/all_gather | solution.py:46
  7.9 206.7 %all-gather.5.cloned.1.call-start = ((), (), s32[]{:S(2)}) async-start(), calls=%async_computation.1 | async-start | bytes 31195136 | tf_op jit(solution)/shard_map/all_gather | solution.py:43
  229.3 9.1 %copy-start.3 = (s32[1,4]{1,0:T(1,128)S(1)}, s32[1,4]{1,0:T(1,128)}, u32[]{:S(2)}) copy-start(s32[1,4]{1,0:T(1,128)} %param.8) | copy-start | bytes 52
  231.0 38.0 %all-to-all-start = ((bf16[16,256,288]{1,2,0:T(8,128)(2,1)}), bf16[16,256,288]{1,2,0:T(8,128)(2,1)S(1)}, u32[]{:S(2)}, u32[]{:S(2)}) async-start(bf16[16,256,288]{1,2,0:T(8,128)(2,1)} %bitcast.85), calls=%async_computation | async-start | bytes 4718592 | tf_op jit(solution)/shard_map/all_to_all | solution.py:52
  238.2 109.2 %all-gather.7.cloned.1.call-start = ((), (), s32[]{:S(2)}) async-start(), calls=%async_computation.2 | async-start | bytes 8912896 | tf_op jit(solution)/shard_map/all_gather | solution.py:109
  270.0 1.4 copy-start
  364.4 8.4 %copy-start.1 = (f32[4,7,256,128]{3,2,1,0:T(8,128)S(1)}, f32[4,7,256,128]{3,2,1,0:T(8,128)}, u32[]{:S(2)}) copy-start(f32[4,7,256,128]{3,2,1,0:T(8,128)} %get-tuple-element.253) | copy-start | bytes 11010052 | tf_op jit(solution)/shard_map/while
  380.7 1.9 copy-start.2
  392.1 8.4 %copy-start.1 = (f32[4,7,256,128]{3,2,1,0:T(8,128)S(1)}, f32[4,7,256,128]{3,2,1,0:T(8,128)}, u32[]{:S(2)}) copy-start(f32[4,7,256,128]{3,2,1,0:T(8,128)} %get-tuple-element.253) | copy-start | bytes 11010052 | tf_op jit(solution)/shard_map/while
  408.5 1.9 copy-start.2
  419.8 8.4 %copy-start.1 = (f32[4,7,256,128]{3,2,1,0:T(8,128)S(1)}, f32[4,7,256,128]{3,2,1,0:T(8,128)}, u32[]{:S(2)}) copy-start(f32[4,7,256,128]{3,2,1,0:T(8,128)} %get-tuple-element.253) | copy-start | bytes 11010052 | tf_op jit(solution)/shard_map/while
  436.2 1.9 copy-start.2
  447.6 8.4 %copy-start.1 = (f32[4,7,256,128]{3,2,1,0:T(8,128)S(1)}, f32[4,7,256,128]{3,2,1,0:T(8,128)}, u32[]{:S(2)}) copy-start(f32[4,7,256,128]{3,2,1,0:T(8,128)} %get-tuple-element.253) | copy-start | bytes 11010052 | tf_op jit(solution)/shard_map/while
  464.0 1.9 copy-start.2
  475.3 8.4 %copy-start.1 = (f32[4,7,256,128]{3,2,1,0:T(8,128)S(1)}, f32[4,7,256,128]{3,2,1,0:T(8,128)}, u32[]{:S(2)}) copy-start(f32[4,7,256,128]{3,2,1,0:T(8,128)} %get-tuple-element.253) | copy-start | bytes 11010052 | tf_op jit(solution)/shard_map/while
  491.7 1.9 copy-start.2
  503.1 8.4 %copy-start.1 = (f32[4,7,256,128]{3,2,1,0:T(8,128)S(1)}, f32[4,7,256,128]{3,2,1,0:T(8,128)}, u32[]{:S(2)}) copy-start(f32[4,7,256,128]{3,2,1,0:T(8,128)} %get-tuple-element.253) | copy-start | bytes 11010052 | tf_op jit(solution)/shard_map/while
  519.5 1.9 copy-start.2
  530.8 8.4 %copy-start.1 = (f32[4,7,256,128]{3,2,1,0:T(8,128)S(1)}, f32[4,7,256,128]{3,2,1,0:T(8,128)}, u32[]{:S(2)}) copy-start(f32[4,7,256,128]{3,2,1,0:T(8,128)} %get-tuple-element.253) | copy-start | bytes 11010052 | tf_op jit(solution)/shard_map/while
  547.2 1.9 copy-start.2
  558.6 8.4 %copy-start.1 = (f32[4,7,256,128]{3,2,1,0:T(8,128)S(1)}, f32[4,7,256,128]{3,2,1,0:T(8,128)}, u32[]{:S(2)}) copy-start(f32[4,7,256,128]{3,2,1,0:T(8,128)} %get-tuple-element.253) | copy-start | bytes 11010052 | tf_op jit(solution)/shard_map/while
  575.0 1.9 copy-start.2
Sparse Core Ops, SparseCore 0:
  9.7 27.8 all-gather.8
  40.3 174.2 all-gather.4
  270.1 77.2 all-gather.6
where the time goes:
time: 597 us; the launch traced here: 593 us
  waiting for transfers between devices  293 us (49%)
  matrix products  131 us (22%)
  other arithmetic  87.5 us (15%)
  local copies, waits for them, and re-layouts  59.5 us (10%)
  between operations  13.9 us (2%)
  starting transfers between devices  7.52 us (1%)
    all_gather x1, waiting for transfers between devices, project_joined(): grouped = lax.all_gather(normed, 'gy', axis=0, tiled=True)  170 us
    all_gather x1, waiting for transfers between devices, on_device(): piece = lax.all_gather(kv_rows, 'gy', axis=0, tiled=True)  68.2 us
    reduce_sum x8, other arithmetic, attend(): total = total * shrink + jnp.sum(weights, axis=3)  66.5 us
    dot_general x8, matrix products, attend(): jnp.einsum('ghrn,ngo->ghro', weights.astype(jnp.bfloat16), value_part, pr...  64.3 us
    dot_general x8, matrix products, attend(): jnp.einsum('rgho,ngo->ghrn', queries, key_part, preferred_element_type=jn...  52.3 us
    all_to_all x1, waiting for transfers between devices, project_joined(): lax.all_to_all(block_out, 'gy', split_axis=0, concat_axis=1, tiled=True)  29.9 us
    all_gather x1, waiting for transfers between devices, project_joined(): lax.all_gather(weight, 'gx', axis=0, tiled=True)  23.6 us
    while x40, local copies, waits for them, and re-layouts  15 us
  transfers between devices with their start and end apart: 4, of which 4 were waited for; matrix products, arithmetic and copies ran while one was open for 4% of the time, Pallas kernels for 0%

commit v1 on v0

--- a/solution.py
+++ b/solution.py
@@ -4,13 +4,102 @@
 import jax.numpy as jnp
 from jax import lax
 from jax.sharding import PartitionSpec as P
+from jax.experimental import pallas as pl
+from jax.experimental.pallas import tpu as pltpu
 
 HEADS = 28
 KV_HEADS = 4
 HEAD_DIM = 128
 
 
-key_span = 512
+BLOCK = 256
+
+
+def flash_body(meta, q_ref, k_ref, v_ref, o_ref, m_ref, l_ref, acc_ref):
+    step = pl.program_id(1)
+    last = pl.num_programs(1) - 1
+    first = meta[4] * BLOCK
+    block = jnp.minimum(meta[5] + step, meta[4])
+    group = HEADS // KV_HEADS
+
+    @pl.when(step == 0)
+    def _():
+        m_ref[...] = jnp.full(m_ref.shape, -1e30, jnp.float32)
+        l_ref[...] = jnp.zeros(l_ref.shape, jnp.float32)
+        acc_ref[...] = jnp.zeros(acc_ref.shape, jnp.float32)
+
+    @pl.when(meta[5] + step <= meta[4])
+    def _():
+        qrow = first + lax.broadcasted_iota(jnp.int32, (BLOCK, BLOCK), 0)
+        kcol = block * BLOCK + lax.broadcasted_iota(jnp.int32, (BLOCK, BLOCK), 1)
+        qstart = jnp.zeros((BLOCK, BLOCK), jnp.int32)
+        for s in range(4):
+            end = meta[s]
+            qstart = jnp.where(end <= qrow, end, qstart)
+        allowed = (kcol >= qstart) & (kcol <= qrow)
+        keys = k_ref[...]
+        values = v_ref[...]
+        scale = 1.0 / HEAD_DIM**0.5
+        for h in range(group):
+            q = q_ref[:, h * HEAD_DIM : (h + 1) * HEAD_DIM]
+            scores = (
+                lax.dot_general(
+                    q, keys, (((1,), (1,)), ((), ())), preferred_element_type=jnp.float32
+                )
+                * scale
+            )
+            m_prev = m_ref[h][:, :1]
+            m_cur = jnp.max(jnp.where(allowed, scores, -1e30), axis=1, keepdims=True)
+            m_new = jnp.maximum(m_prev, m_cur)
+            shrink = jnp.exp(m_prev - m_new)
+            weights = jnp.where(allowed, jnp.exp(scores - m_new), 0.0)
+            l_new = l_ref[h][:, :1] * shrink + jnp.sum(weights, axis=1, keepdims=True)
+            acc_ref[h] = acc_ref[h] * shrink + jnp.dot(
+                weights.astype(jnp.bfloat16), values, preferred_element_type=jnp.float32
+            )
+            m_ref[h] = jnp.broadcast_to(m_new, (BLOCK, HEAD_DIM))
+            l_ref[h] = jnp.broadcast_to(l_new, (BLOCK, HEAD_DIM))
+
+    @pl.when(step == last)
+    def _():
+        for h in range(group):
+            o_ref[:, h * HEAD_DIM : (h + 1) * HEAD_DIM] = (
+                acc_ref[h] / l_ref[h][:, :1]
+            ).astype(o_ref.dtype)
+
+
+def flash(meta, queries, kv_all, steps):
+    rows = queries.shape[0]
+    group = HEADS // KV_HEADS
+    width = group * HEAD_DIM
+
+    def key_map(g, t, meta):
+        return (jnp.minimum(meta[5] + t, meta[4]), g)
+
+    def value_map(g, t, meta):
+        return (jnp.minimum(meta[5] + t, meta[4]), KV_HEADS + g)
+
+    spec = pltpu.PrefetchScalarGridSpec(
+        num_scalar_prefetch=1,
+        grid=(KV_HEADS, steps),
+        in_specs=[
+            pl.BlockSpec((rows, width), lambda g, t, meta: (0, g)),
+            pl.BlockSpec((BLOCK, HEAD_DIM), key_map),
+            pl.BlockSpec((BLOCK, HEAD_DIM), value_map),
+        ],
+        out_specs=pl.BlockSpec((rows, width), lambda g, t, meta: (0, g)),
+        scratch_shapes=[
+            pltpu.VMEM((group, rows, HEAD_DIM), jnp.float32),
+            pltpu.VMEM((group, rows, HEAD_DIM), jnp.float32),
+            pltpu.VMEM((group, rows, HEAD_DIM), jnp.float32),
+        ],
+    )
+    return pl.pallas_call(
+        flash_body,
+        grid_spec=spec,
+        out_shape=jax.ShapeDtypeStruct((rows, HEADS * HEAD_DIM), jnp.bfloat16),
+        compiler_params=pltpu.CompilerParams(dimension_semantics=("arbitrary", "arbitrary")),
+    )(meta, queries, kv_all, kv_all)
 
 
 def norm_rows(values, gain):
@@ -70,58 +159,13 @@
     queries = rotate(joined[:, :qdim], pos, HEADS).reshape(rows, KV_HEADS, group, HEAD_DIM)
     keys = rotate(joined[:, qdim : qdim + kdim], pos, KV_HEADS)
     kv_rows = jnp.concatenate([keys, joined[:, qdim + kdim :]], axis=1)
-    scale = 1.0 / HEAD_DIM**0.5
-
-    def attend(carry, piece, start):
-        running, total, summed = carry
-        key_count = piece.shape[0]
-        key_index = start + jnp.arange(key_count, dtype=jnp.int32)
-        key_seg = segment_of(key_index, ends)
-        key_part = piece[:, :kdim].reshape(key_count, KV_HEADS, HEAD_DIM)
-        value_part = piece[:, kdim:].reshape(key_count, KV_HEADS, HEAD_DIM)
-        scores = (
-            jnp.einsum("rgho,ngo->ghrn", queries, key_part, preferred_element_type=jnp.float32)
-            * scale
-        )
-        allowed = (seg_here[:, None] == key_seg[None, :]) & (
-            key_index[None, :] <= tokens_here[:, None]
-        )
-        newest = jnp.maximum(running, jnp.max(jnp.where(allowed, scores, -1e30), axis=3))
-        shrink = jnp.exp(running - newest)
-        weights = jnp.where(allowed, jnp.exp(scores - newest[..., None]), 0.0)
-        total = total * shrink + jnp.sum(weights, axis=3)
-        summed = summed * shrink[..., None] + jnp.einsum(
-            "ghrn,ngo->ghro",
-            weights.astype(jnp.bfloat16),
-            value_part,
-            preferred_element_type=jnp.float32,
-        )
-        return (newest, total, summed)
-
-    def visit(carry, piece, start):
-        return attend(carry, piece, start)
-
-    start_state = (
-        jnp.full((KV_HEADS, group, rows), -1e30, jnp.float32),
-        jnp.zeros((KV_HEADS, group, rows), jnp.float32),
-        jnp.zeros((KV_HEADS, group, rows, HEAD_DIM), jnp.float32),
-    )
     piece = lax.all_gather(kv_rows, "gy", axis=0, tiled=True)
-    length = piece.shape[0]
-    span = math.gcd(length, key_span)
-    stacked = piece.reshape(length // span, span, piece.shape[1])
-    offsets = jnp.arange(length // span, dtype=jnp.int32) * span
-
-    def advance(state, item):
-        return (visit(state, item[0], item[1]), None)
-
-    final_state, unused = lax.scan(advance, start_state, (stacked, offsets))
-    running, total, summed = final_state
-    attn = (
-        jnp.transpose(summed / total[..., None], (2, 0, 1, 3))
-        .reshape(rows, qdim)
-        .astype(jnp.bfloat16)
-    )
+    lead = jnp.max(jnp.where(ends <= first, ends, 0))
+    meta = jnp.concatenate(
+        [ends, jnp.stack([lax.axis_index("gy"), lead // BLOCK, 0, 0]).astype(jnp.int32)]
+    ).astype(jnp.int32)
+    steps = min(piece.shape[0] // BLOCK, 9)
+    attn = flash(meta, queries.reshape(rows, qdim), piece, steps)
     return (attn, kv_rows)
 
 

time: 597 us -> 497 us (0.83)
  the two profiles are of different devices: /device:TPU:28 before, /device:TPU:29 now
where the time goes in v1:
time: 497 us; the launch traced here: 496 us
  waiting for transfers between devices  288 us (58%)
  Pallas kernels  143 us (29%)
  local copies, waits for them, and re-layouts  17.2 us (3%)
  between operations  16.5 us (3%)
  matrix products  14.7 us (3%)
  other arithmetic  9.97 us (2%)
  starting transfers between devices  7.09 us (1%)
    all_gather x1, waiting for transfers between devices, project_joined(): grouped = lax.all_gather(normed, 'gy', axis=0, tiled=True)  170 us
    pallas_call x1, Pallas kernels, flash(): pl.pallas_call(flash_body, grid_spec=spec, out_shape=jax.ShapeDtypeStruct...  143 us
    all_gather x1, waiting for transfers between devices, on_device(): piece = lax.all_gather(kv_rows, 'gy', axis=0, tiled=True)  63.1 us
    all_to_all x1, waiting for transfers between devices, project_joined(): lax.all_to_all(block_out, 'gy', split_axis=0, concat_axis=1, tiled=True)  29.3 us
    all_gather x1, waiting for transfers between devices, project_joined(): lax.all_gather(weight, 'gx', axis=0, tiled=True)  24.8 us
    dot_general x1, matrix products, project_joined(): jnp.dot(grouped, lax.all_gather(weight, 'gx', axis=0, tiled=True), prefer...  14.7 us
  transfers between devices with their start and end apart: 4, of which 4 were waited for; matrix products, arithmetic and copies ran while one was open for 4% of the time, Pallas kernels for 0%

profile of v1, /device:TPU:29, one launch (start us, length us, event | category | flops | bytes accessed | tf_op | source)
XLA Modules:
  0.0 496.4 jit_solution(13164584784396228504)
XLA Ops:
  7.2 0.7 all-gather.9.cloned.1.call-update
  8.0 1.9 fusion.1
  9.9 2.5 fusion.3
  12.4 0.8 dynamic_slice.3
  13.2 24.8 %all-gather.9.cloned.1.call-done = bf16[8,448,288]{1,2,0:T(8,128)(2,1)} async-done(((bf16[1,448,288]{1,2,0:T(8,128)(2,1)}), bf16[8,448,288]{1,2,0:T(8,128)(2,1)}) %all-gather.9.cloned.1.call-update) | async-done | bytes 2064400 | tf_op jit(solution)/shard_map/all_gather | solution.py:135
  38.0 3.0 copy.24
  40.9 3.6 reshape.143
  44.5 169.9 %all-gather.5.cloned.1.call-done = bf16[4096,3584]{1,0:T(8,128)(2,1)} async-done(((bf16[256,3584]{1,0:T(8,128)(2,1)}), bf16[4096,3584]{1,0:T(8,128)(2,1)}) %all-gather.5.cloned.1.call-update) | async-done | bytes 29360144 | tf_op jit(solution)/shard_map/all_gather | solution.py:132
  214.4 14.7 %fusion = bf16[4096,288]{0,1:T(8,128)(2,1)S(1)} fusion(bf16[4096,3584]{1,0:T(8,128)(2,1)} %all-gather.5.cloned.1.call-done, bf16[3584,288]{0,1:T(8,128)(2,1)} %reshape.143, f32[288]{0:T(512)S(1)} %dynamic_slice.3), kind=kOutput, calls=%fused_computation.1 | convolution fusion | flops 8458076160 | bytes 33784960 | tf_op jit(solution)/shard_map/dot_general | solution.py:133
  229.1 1.7 copy.39
  230.8 6.8 %all-to-all-start = ((bf16[16,256,288]{1,2,0:T(8,128)(2,1)}), bf16[16,256,288]{1,2,0:T(8,128)(2,1)S(1)}, u32[]{:S(2)}, u32[]{:S(2)}) async-start(bf16[16,256,288]{1,2,0:T(8,128)(2,1)} %bitcast.29), calls=%async_computation | async-start | bytes 4718592 | tf_op jit(solution)/shard_map/all_to_all | solution.py:141
  237.6 0.2 all-gather.7.cloned.1.call-start
  237.8 0.2 reduce-window.8
  238.1 0.3 multiply_cosine_fusion
  238.4 0.7 copy.27
  239.2 0.8 copy.29
  239.9 29.3 %all-to-all-done = bf16[16,256,288]{1,2,0:T(8,128)(2,1)S(1)} async-done(((bf16[16,256,288]{1,2,0:T(8,128)(2,1)}), bf16[16,256,288]{1,2,0:T(8,128)(2,1)S(1)}, u32[]{:S(2)}, u32[]{:S(2)}) %all-to-all-start) | async-done | bytes 2359328 | tf_op jit(solution)/shard_map/all_to_all | solution.py:141
  269.2 0.7 fusion.5
  270.0 0.7 fusion.6
  270.7 0.2 copy.32
  270.9 1.2 copy.33
  272.1 1.2 subtract_convert_fusion.1
  273.4 0.4 pad_maximum_fusion.2
  273.8 1.1 copy.34
  274.9 0.9 pad_maximum_fusion.1
  275.8 0.6 fusion.4
  279.0 0.6 pad_add_fusion.meta
  279.8 0.4 convert.18
  280.2 0.6 subtract_convert_fusion
  281.0 2.6 copy.31.q_ref
  283.6 63.1 %all-gather.7.cloned.1.call-done.k_ref.v_ref = bf16[4096,1024]{1,0:T(8,128)(2,1)} async-done(((bf16[256,1024]{1,0:T(8,128)(2,1)}), bf16[4096,1024]{1,0:T(8,128)(2,1)}) %all-gather.7.cloned.1.call-update) | async-done | bytes 8388624 | tf_op jit(solution)/shard_map/all_gather | solution.py:162
  346.8 143.1 %shard_map.68 = bf16[256,3584]{1,0:T(8,128)(2,1)} custom-call(s32[8]{0:T(128)} %pad_add_fusion.meta, bf16[256,3584]{1,0:T(8,128)(2,1)} %copy.31.q_ref, bf16[4096,1024]{1,0:T(8,128)(2,1)} %all-gather.7.cloned.1.call-done.k_ref.v_ref, bf16[4096,1024]{1,0:T(8,128)(2,1)} %all-gather.7.cloned.1.call-done.k_ref.v_ref), custom_call_target="tpu_custom_call" | custom-call | tf_op jit(solution)/shard_map/pallas_call | solution.py:97
  (17 shorter events, 0.6 us)
Async XLA Ops:
  7.2 2.7 copy-start
  7.2 30.8 %all-gather.9.cloned.1.call-start = ((), (), s32[]{:S(2)}) async-start(), calls=%async_computation.3 | async-start | bytes 2654208 | tf_op jit(solution)/shard_map/all_gather | solution.py:135
  7.9 206.5 %all-gather.5.cloned.1.call-start = ((), (), s32[]{:S(2)}) async-start(), calls=%async_computation.1 | async-start | bytes 31195136 | tf_op jit(solution)/shard_map/all_gather | solution.py:132
  230.8 7.0 %copy-start.1 = (s32[1,4]{1,0:T(1,128)S(1)}, s32[1,4]{1,0:T(1,128)}, u32[]{:S(2)}) copy-start(s32[1,4]{1,0:T(1,128)} %param.6) | copy-start | bytes 52
  230.8 38.4 %all-to-all-start = ((bf16[16,256,288]{1,2,0:T(8,128)(2,1)}), bf16[16,256,288]{1,2,0:T(8,128)(2,1)S(1)}, u32[]{:S(2)}, u32[]{:S(2)}) async-start(bf16[16,256,288]{1,2,0:T(8,128)(2,1)} %bitcast.29), calls=%async_computation | async-start | bytes 4718592 | tf_op jit(solution)/shard_map/all_to_all | solution.py:141
  237.6 109.2 %all-gather.7.cloned.1.call-start = ((), (), s32[]{:S(2)}) async-start(), calls=%async_computation.2 | async-start | bytes 8912896 | tf_op jit(solution)/shard_map/all_gather | solution.py:162
Sparse Core Ops, SparseCore 0:
  9.7 28.2 all-gather.8
  40.7 173.7 all-gather.4
  275.9 70.8 all-gather.6
